TPU v7x, 32 devices: a whole 2x2x4 slice. The times are simulated.
32 devices in a mesh: row: 8 (over z, x), col: 4 (over y, core).
Axes of the slice: x: 2, y: 2, z: 4, core: 2. Of those that a mesh axis runs over, the one named last changes fastest.
Arguments:
- low_rhs: bfloat16 [32, 512, 128], P(('row', 'col')), may hold values from -6 to 6
- low_inv: bfloat16 [32, 512, 512], P(('row', 'col'))
- low_tiles: bfloat16 [32, 4, 512, 512], P(('row', 'col')), may hold values from -0.03125 to 0.03125
- tile_rows: int32 [32, 4], P(('row', 'col')), may hold values from -1 to 3, as said below
- tile_cols: int32 [32, 4], P(('row', 'col')), may hold values from 0 to 31, as said below
- top_rhs: bfloat16 [4, 512, 128], P(None, 'row'), may hold values from -6 to 6
- top_inv: bfloat16 [4, 512, 512], P(None, 'row')
- top_tiles: bfloat16 [6, 512, 512], P(None, 'row'), may hold values from -0.125 to 0.125
Outputs:
- low_solution: float32 [32, 512, 128], P(('row', 'col'))
- top_solution: float32 [4, 512, 128], P(None, 'row')
Inputs may be any that keep to these rules, and one draw needn't show every extreme that they name: `tile_rows`: in each block's list of 4 slots the used slots come first and name top-level blocks; the remaining slots hold -1. Some list has only its first slot used and some list is full. Slot s of block j names a block of j's aligned group of 4 blocks (j // 4 == tile_cols[j, s] // 4); an empty slot names j itself.
All inputs are finite; a program needn't handle non-finite values.
Results may differ from a plain program's by a relative error of at most 0.022.
Values may be sent and summed in bfloat16 or wider, within the bound.
No kernel may reach another device: no remote copies, remote signals or barrier semaphores. Data moves between devices by JAX's collectives and lax.ppermute only.
A program may use at most 64 MiB of HBM per device.

v0:
```python
import jax
import jax.numpy as jnp
from jax import lax
from jax.sharding import PartitionSpec as P


def local(low_rhs, low_inv, low_tiles, tile_rows, tile_cols, top_rhs, top_inv, top_tiles):
    peers = lax.axis_size("col")
    levels = top_rhs.shape[0]
    share = top_rhs.shape[1]
    position = lax.axis_index("row")
    slot_rows = tile_rows[0]
    slot_cols = tile_cols[0] % peers
    alive = slot_rows >= 0
    safe_rows = jnp.maximum(slot_rows, 0)
    own_tiles = low_tiles[0]
    low_forward = jnp.dot(low_inv[0], low_rhs[0], preferred_element_type=jnp.float32).astype(
        jnp.bfloat16
    )
    panels = lax.all_gather(low_forward[None], "col", axis=0, tiled=True)
    products = jnp.einsum(
        "sab,sbk->sak", own_tiles, panels[slot_cols], preferred_element_type=jnp.float32
    )
    pick_level = (slot_rows[:, None] == jnp.arange(levels, dtype=jnp.int32)[None, :]).astype(
        jnp.float32
    )
    coupling = jnp.einsum("st,sak->tak", pick_level, products, precision=lax.Precision.HIGHEST)
    whole_sum = lax.psum(coupling.astype(jnp.bfloat16), "col")
    coupled = lax.psum_scatter(whole_sum, "row", scatter_dimension=1, tiled=True).astype(
        jnp.float32
    )
    top_back = [None] * levels
    top_slices = [None] * levels
    top_forward = []
    for level in range(levels):
        residue = top_rhs[level].astype(jnp.float32) - coupled[level]
        if level > 0:
            first = level * (level - 1) // 2
            earlier = jnp.stack(top_forward)
            residue = residue - jnp.einsum(
                "uab,ubk->ak",
                top_tiles[first : first + level],
                earlier,
                preferred_element_type=jnp.float32,
            )
        whole_residue = lax.all_gather(residue.astype(jnp.bfloat16), "row", axis=0, tiled=True)
        solved_part = jnp.dot(
            top_inv[level], whole_residue, preferred_element_type=jnp.float32
        ).astype(jnp.bfloat16)
        top_forward.append(lax.all_gather(solved_part, "row", axis=0, tiled=True))
    for level in reversed(range(levels)):
        update = lax.dynamic_slice_in_dim(top_forward[level], position * share, share, 0).astype(
            jnp.float32
        )
        if level < levels - 1:
            later = list(range(level + 1, levels))
            tiles_below = jnp.stack([top_tiles[k * (k - 1) // 2 + level] for k in later])
            slices_below = jnp.stack(
                [lax.dynamic_slice_in_dim(top_back[k], position * share, share, 0) for k in later]
            )
            partial_term = jnp.einsum(
                "kab,kac->bc", tiles_below, slices_below, preferred_element_type=jnp.float32
            )
            update = update - lax.psum_scatter(
                partial_term.astype(jnp.bfloat16), "row", scatter_dimension=0, tiled=True
            ).astype(jnp.float32)
        local_part = jnp.einsum(
            "ab,ac->bc",
            top_inv[level],
            update.astype(jnp.bfloat16),
            preferred_element_type=jnp.float32,
        )
        solution = lax.psum(local_part.astype(jnp.bfloat16), "row").astype(jnp.float32)
        top_slices[level] = lax.dynamic_slice_in_dim(solution, position * share, share, 0)
        top_back[level] = solution.astype(jnp.bfloat16)
    back_stack = jnp.stack(top_back)
    products_back = jnp.einsum(
        "sab,sak->sbk", own_tiles, back_stack[safe_rows], preferred_element_type=jnp.float32
    )
    pick_peer = (
        (slot_cols[:, None] == jnp.arange(peers, dtype=jnp.int32)[None, :]) & alive[:, None]
    ).astype(jnp.float32)
    terms = jnp.einsum("sp,sbk->pbk", pick_peer, products_back, precision=lax.Precision.HIGHEST)
    returned = lax.psum_scatter(
        terms.astype(jnp.bfloat16), "col", scatter_dimension=0, tiled=True
    ).astype(jnp.float32)
    low_update = (low_forward.astype(jnp.float32) - returned[0]).astype(jnp.bfloat16)
    low_solution = jnp.einsum(
        "ab,ac->bc", low_inv[0], low_update, preferred_element_type=jnp.float32
    )
    return (low_solution[None], jnp.stack(top_slices))


def solution(mesh):
    in_specs = (
        P(("row", "col"), None, None),
        P(("row", "col"), None, None),
        P(("row", "col"), None, None, None),
        P(("row", "col"), None),
        P(("row", "col"), None),
        P(None, "row", None),
        P(None, "row", None),
        P(None, "row", None),
    )
    out_specs = (P(("row", "col"), None, None), P(None, "row", None))
    return jax.shard_map(local, mesh=mesh, in_specs=in_specs, out_specs=out_specs, check_vma=False)
```

profile of v0, /device:TPU:0, one launch (start us, length us, event | category | flops | bytes accessed | tf_op | source)
XLA Modules:
  0.0 905.1 jit_solution(3152110872918101658)
XLA Ops:
  8.7 8.7 all-gather
  19.5 1.9 fusion.4
  22.7 3.2 convolution_convert_fusion
  27.2 72.4 %all-reduce.18.cloned.1.call-done = bf16[4,512,128]{2,0,1:T(4,128)(2,1)} async-done(((bf16[4,512,128]{2,0,1:T(4,128)(2,1)}), bf16[4,512,128]{2,0,1:T(4,128)(2,1)}) %all-reduce.18.cloned.1.call-update) | async-done | bytes 524304
  101.2 32.1 %all-reduce.16.cloned.1.call-done = bf16[4,64,128]{2,1,0:T(8,128)(2,1)} async-done(((bf16[4,64,128]{2,1,0:T(8,128)(2,1)}), bf16[4,64,128]{2,1,0:T(8,128)(2,1)}) %all-reduce.16.cloned.1.call-update) | async-done | bytes 65552 | tf_op jit(solution)/shard_map/psum | solution.py:28
  134.1 30.7 %all-gather.1 = bf16[1,512,128]{2,1,0:T(8,128)(2,1)S(1)} all-gather(bf16[1,64,128]{2,1,0:T(8,128)(2,1)S(1)} %fusion.76), channel_id=3, replica_groups=mesh['row'=8,'col'=4] {'row'}, dimensions={1}, use_global_device_ids=true | all-gather | bytes 147456 | tf_op jit(solution)/shard_map/all_gather | solution.py:46
  164.9 30.6 %all_gather.29 = bf16[512,128]{1,0:T(8,128)(2,1)S(1)} all-gather(bf16[64,128]{1,0:T(8,128)(2,1)S(1)} %fusion.23), channel_id=1, replica_groups=mesh['row'=8,'col'=4] {'row'}, dimensions={0}, use_global_device_ids=true | all-gather | bytes 147456 | tf_op jit(solution)/shard_map/all_gather | solution.py:50
  195.6 30.5 %all_gather.30 = bf16[512,128]{1,0:T(8,128)(2,1)S(1)} all-gather(bf16[64,128]{1,0:T(8,128)(2,1)S(1)} %fusion.20), channel_id=1, replica_groups=mesh['row'=8,'col'=4] {'row'}, dimensions={0}, use_global_device_ids=true | all-gather | bytes 147456 | tf_op jit(solution)/shard_map/all_gather | solution.py:46
  226.3 30.6 %all_gather.31 = bf16[512,128]{1,0:T(8,128)(2,1)S(1)} all-gather(bf16[64,128]{1,0:T(8,128)(2,1)S(1)} %fusion.24), channel_id=1, replica_groups=mesh['row'=8,'col'=4] {'row'}, dimensions={0}, use_global_device_ids=true | all-gather | bytes 147456 | tf_op jit(solution)/shard_map/all_gather | solution.py:50
  257.1 30.6 %all_gather.32 = bf16[512,128]{1,0:T(8,128)(2,1)S(1)} all-gather(bf16[64,128]{1,0:T(8,128)(2,1)S(1)} %fusion.22), channel_id=1, replica_groups=mesh['row'=8,'col'=4] {'row'}, dimensions={0}, use_global_device_ids=true | all-gather | bytes 147456 | tf_op jit(solution)/shard_map/all_gather | solution.py:46
  287.8 30.6 %all_gather.33 = bf16[512,128]{1,0:T(8,128)(2,1)S(1)} all-gather(bf16[64,128]{1,0:T(8,128)(2,1)S(1)} %fusion.25), channel_id=1, replica_groups=mesh['row'=8,'col'=4] {'row'}, dimensions={0}, use_global_device_ids=true | all-gather | bytes 147456 | tf_op jit(solution)/shard_map/all_gather | solution.py:50
  319.4 30.5 %all_gather.34 = bf16[512,128]{1,0:T(8,128)(2,1)S(1)} all-gather(bf16[64,128]{1,0:T(8,128)(2,1)S(1)} %fusion.21), channel_id=1, replica_groups=mesh['row'=8,'col'=4] {'row'}, dimensions={0}, use_global_device_ids=true | all-gather | bytes 147456 | tf_op jit(solution)/shard_map/all_gather | solution.py:46
  350.1 30.5 %all_gather.35 = bf16[512,128]{1,0:T(8,128)(2,1)S(1)} all-gather(bf16[64,128]{1,0:T(8,128)(2,1)S(1)} %fusion.26), channel_id=1, replica_groups=mesh['row'=8,'col'=4] {'row'}, dimensions={0}, use_global_device_ids=true | all-gather | bytes 147456 | tf_op jit(solution)/shard_map/all_gather | solution.py:50
  381.5 70.7 %all-reduce.8.cloned.1.call-done = bf16[512,128]{0,1:T(8,128)(2,1)} async-done(((bf16[512,128]{0,1:T(8,128)(2,1)}), bf16[512,128]{0,1:T(8,128)(2,1)}) %all-reduce.8.cloned.1.call-update) | async-done | bytes 131088 | tf_op jit(solution)/shard_map/psum | solution.py:73
  454.1 62.9 %reduce-scatter.5.cloned.1.call-done = bf16[64,128]{1,0:T(8,128)(2,1)} async-done(((bf16[512,128]{1,0:T(8,128)(2,1)}), bf16[64,128]{1,0:T(8,128)(2,1)}) %reduce-scatter.5.cloned.1.call-update) | async-done | bytes 16400 | tf_op jit(solution)/shard_map/reduce_scatter | solution.py:64
  519.3 70.9 %all-reduce.10.cloned.1.call-done = bf16[512,128]{0,1:T(8,128)(2,1)} async-done(((bf16[512,128]{0,1:T(8,128)(2,1)}), bf16[512,128]{0,1:T(8,128)(2,1)}) %all-reduce.10.cloned.1.call-update) | async-done | bytes 131088 | tf_op jit(solution)/shard_map/psum | solution.py:73
  591.3 1.8 fusion.10
  593.1 61.9 %reduce-scatter.7.cloned.1.call-done = bf16[64,128]{1,0:T(8,128)(2,1)} async-done(((bf16[512,128]{1,0:T(8,128)(2,1)}), bf16[64,128]{1,0:T(8,128)(2,1)}) %reduce-scatter.7.cloned.1.call-update) | async-done | bytes 16400 | tf_op jit(solution)/shard_map/reduce_scatter | solution.py:64
  656.7 71.8 %all-reduce.12.cloned.1.call-done = bf16[512,128]{0,1:T(8,128)(2,1)} async-done(((bf16[512,128]{0,1:T(8,128)(2,1)}), bf16[512,128]{0,1:T(8,128)(2,1)}) %all-reduce.12.cloned.1.call-update) | async-done | bytes 131088 | tf_op jit(solution)/shard_map/psum | solution.py:73
  729.4 1.8 fusion.11
  731.3 62.1 %reduce-scatter.9.cloned.1.call-done = bf16[64,128]{1,0:T(8,128)(2,1)} async-done(((bf16[512,128]{1,0:T(8,128)(2,1)}), bf16[64,128]{1,0:T(8,128)(2,1)}) %reduce-scatter.9.cloned.1.call-update) | async-done | bytes 16400 | tf_op jit(solution)/shard_map/reduce_scatter | solution.py:64
  795.1 71.8 %all-reduce.14.cloned.1.call-done = bf16[512,128]{0,1:T(8,128)(2,1)} async-done(((bf16[512,128]{0,1:T(8,128)(2,1)}), bf16[512,128]{0,1:T(8,128)(2,1)}) %all-reduce.14.cloned.1.call-update) | async-done | bytes 131088 | tf_op jit(solution)/shard_map/psum | solution.py:73
  872.1 2.4 fusion.90
  877.3 19.0 %reduce-scatter.11.cloned.1.call-done = bf16[1,512,128]{2,1,0:T(8,128)(2,1)} async-done(((bf16[4,512,128]{2,1,0:T(8,128)(2,1)}), bf16[1,512,128]{2,1,0:T(8,128)(2,1)}) %reduce-scatter.11.cloned.1.call-update) | async-done | bytes 131088 | tf_op jit(solution)/shard_map/reduce_scatter | solution.py:84
  (102 shorter events, 30.4 us)
Async XLA Ops:
  7.2 12.3 %copy-start = (bf16[1,4,512,512]{3,2,1,0:T(8,128)(2,1)S(1)}, bf16[1,4,512,512]{3,2,1,0:T(8,128)(2,1)}, u32[]{:S(2)}) copy-start(bf16[1,4,512,512]{3,2,1,0:T(8,128)(2,1)} %param.10) | copy-start | bytes 6291460
  7.2 92.4 %all-reduce.18.cloned.1.call-start = ((), (), s32[]{:S(2)}) async-start(), calls=%async_computation.13 | async-start | bytes 1048576
  21.4 4.6 copy-start.16
  21.4 143.4 %copy-start.2 = (bf16[4,64,512]{2,1,0:T(8,128)(2,1)S(1)}, bf16[4,64,512]{2,1,0:T(8,128)(2,1)}, u32[]{:S(2)}) copy-start(bf16[4,64,512]{2,1,0:T(8,128)(2,1)} %param.14) | copy-start | bytes 786436
  22.7 111.4 %copy-start.13 = (bf16[4,64,128]{2,1,0:T(8,128)(2,1)S(1)}, bf16[4,64,128]{2,1,0:T(8,128)(2,1)}, u32[]{:S(2)}) copy-start(bf16[4,64,128]{2,1,0:T(8,128)(2,1)} %param.13) | copy-start | bytes 196612
  22.7 172.7 %copy-start.3 = (bf16[6,64,512]{2,1,0:T(8,128)(2,1)S(1)}, bf16[6,64,512]{2,1,0:T(8,128)(2,1)}, u32[]{:S(2)}) copy-start(bf16[6,64,512]{2,1,0:T(8,128)(2,1)} %param.15) | copy-start | bytes 1179652
  25.9 107.3 %all-reduce.16.cloned.1.call-start = ((), (), s32[]{:S(2)}) async-start(), calls=%async_computation.12 | async-start | bytes 131072 | tf_op jit(solution)/shard_map/psum | solution.py:28
  101.1 351.1 %all-reduce.8.cloned.1.call-start = ((), (), s32[]{:S(2)}) async-start(), calls=%async_computation.4 | async-start | bytes 262144 | tf_op jit(solution)/shard_map/psum | solution.py:73
  256.9 124.6 %copy-start.12 = (bf16[512,128]{1,0:T(8,128)(2,1)}, bf16[512,128]{1,0:T(8,128)(2,1)S(1)}, u32[]{:S(2)}) copy-start(bf16[512,128]{1,0:T(8,128)(2,1)S(1)} %all_gather.31) | copy-start | bytes 393220
  318.4 411.0 %slice-start = ((bf16[6,64,512]{2,1,0:T(8,128)(2,1)}), bf16[2,64,512]{2,1,0:T(8,128)(2,1)S(1)}, s32[]{:S(2)}) async-start(bf16[6,64,512]{2,1,0:T(8,128)(2,1)} %param.15), calls=%async_computation.14 | async-start | bytes 262144 | tf_op jit(solution)/shard_map/slice | solution.py:57
  319.4 411.9 %copy-start.15 = (s32[1,4]{1,0:T(1,128)S(1)}, s32[1,4]{1,0:T(1,128)}, u32[]{:S(2)}) copy-start(s32[1,4]{1,0:T(1,128)} %param.12) | copy-start | bytes 52
  381.5 135.4 %reduce-scatter.5.cloned.1.call-start = ((), (), s32[]{:S(2)}) async-start(), calls=%async_computation.5 | async-start | bytes 147456 | tf_op jit(solution)/shard_map/reduce_scatter | solution.py:64
  452.2 414.7 %copy-start.10 = (bf16[512,128]{0,1:T(8,128)(2,1)S(1)}, bf16[512,128]{0,1:T(8,128)(2,1)}, u32[]{:S(2)}) copy-start(bf16[512,128]{0,1:T(8,128)(2,1)} %all-reduce.8.cloned.1.call-done) | copy-start | bytes 393220
  453.1 414.8 %copy-start.4 = (bf16[64,128]{0,1:T(8,128)(2,1)}, bf16[64,128]{0,1:T(8,128)(2,1)S(1)}, u32[]{:S(2)}) copy-start(bf16[64,128]{0,1:T(8,128)(2,1)S(1)} %constant_dynamic-slice_fusion.2) | copy-start | bytes 49156
  454.0 136.2 %all-reduce.10.cloned.1.call-start = ((), (), s32[]{:S(2)}) async-start(), calls=%async_computation.6 | async-start | bytes 262144 | tf_op jit(solution)/shard_map/psum | solution.py:73
  518.5 136.5 %reduce-scatter.7.cloned.1.call-start = ((), (), s32[]{:S(2)}) async-start(), calls=%async_computation.7 | async-start | bytes 147456 | tf_op jit(solution)/shard_map/reduce_scatter | solution.py:64
  590.3 276.6 %copy-start.11 = (bf16[512,128]{0,1:T(8,128)(2,1)S(1)}, bf16[512,128]{0,1:T(8,128)(2,1)}, u32[]{:S(2)}) copy-start(bf16[512,128]{0,1:T(8,128)(2,1)} %all-reduce.10.cloned.1.call-done) | copy-start | bytes 393220
  591.2 276.8 %copy-start.6 = (bf16[64,128]{0,1:T(8,128)(2,1)}, bf16[64,128]{0,1:T(8,128)(2,1)S(1)}, u32[]{:S(2)}) copy-start(bf16[64,128]{0,1:T(8,128)(2,1)S(1)} %constant_dynamic-slice_fusion.1) | copy-start | bytes 49156
  593.0 135.4 %all-reduce.12.cloned.1.call-start = ((), (), s32[]{:S(2)}) async-start(), calls=%async_computation.8 | async-start | bytes 262144 | tf_op jit(solution)/shard_map/psum | solution.py:73
  656.6 136.8 %reduce-scatter.9.cloned.1.call-start = ((), (), s32[]{:S(2)}) async-start(), calls=%async_computation.9 | async-start | bytes 147456 | tf_op jit(solution)/shard_map/reduce_scatter | solution.py:64
  729.3 138.6 %copy-start.8 = (bf16[64,128]{0,1:T(8,128)(2,1)}, bf16[64,128]{0,1:T(8,128)(2,1)S(1)}, u32[]{:S(2)}) copy-start(bf16[64,128]{0,1:T(8,128)(2,1)S(1)} %constant_dynamic-slice_fusion) | copy-start | bytes 49156
  731.2 135.7 %all-reduce.14.cloned.1.call-start = ((), (), s32[]{:S(2)}) async-start(), calls=%async_computation.10 | async-start | bytes 262144 | tf_op jit(solution)/shard_map/psum | solution.py:73
  795.0 101.3 %reduce-scatter.11.cloned.1.call-start = ((), (), s32[]{:S(2)}) async-start(), calls=%async_computation.11 | async-start | bytes 655360 | tf_op jit(solution)/shard_map/reduce_scatter | solution.py:84
  872.1 24.2 %copy-start.1 = (bf16[1,512,512]{2,1,0:T(8,128)(2,1)S(1)}, bf16[1,512,512]{2,1,0:T(8,128)(2,1)}, u32[]{:S(2)}) copy-start(bf16[1,512,512]{2,1,0:T(8,128)(2,1)} %param.9) | copy-start | bytes 1572868
  (4 other events, 13.3 us)
Sparse Core Ops, SparseCore 0:
  26.0 73.4 all-reduce.17
  102.5 30.7 all-reduce.15
  381.6 70.5 all-reduce.7
  455.9 60.9 reduce-scatter.4
  520.7 69.5 all-reduce.9
  594.0 60.9 reduce-scatter.6
  658.9 69.5 all-reduce.11
  732.4 60.9 reduce-scatter.8
  797.3 69.5 all-reduce.13
  875.5 20.7 reduce-scatter.10
where the time goes:
time: 906 us; the launch traced here: 905 us
  waiting for transfers between devices  596 us (66%)
  blocking collectives  253 us (28%)
  matrix products  23.5 us (3%)
  between operations  15.1 us (2%)
  local copies, waits for them, and re-layouts  13.2 us (1%)
    psum x4, waiting for transfers between devices, local(): lax.psum(local_part.astype(jnp.bfloat16), 'row').astype(jnp.float32)  285 us
    reduce_scatter x3, waiting for transfers between devices, local(): lax.psum_scatter(partial_term.astype(jnp.bfloat16), 'row', scatter_dimens...  187 us
    all_gather x4, blocking collectives, local(): lax.all_gather(residue.astype(jnp.bfloat16), 'row', axis=0, tiled=True)  122 us
    all_gather x4, blocking collectives, local(): top_forward.append(lax.all_gather(solved_part, 'row', axis=0, tiled=True))  122 us
    unnamed x11, waiting for transfers between devices  72.5 us
    psum x1, waiting for transfers between devices, local(): whole_sum = lax.psum(coupling.astype(jnp.bfloat16), 'col')  32.1 us
    reduce_scatter x1, waiting for transfers between devices, local(): lax.psum_scatter(terms.astype(jnp.bfloat16), 'col', scatter_dimension=0,...  19 us
  transfers between devices with their start and end apart: 10, of which 10 were waited for; matrix products, arithmetic and copies ran while one was open for 0% of the time, Pallas kernels for 0%

commit v1 on v0

--- a/solution.py
+++ b/solution.py
@@ -2,6 +2,19 @@
 import jax.numpy as jnp
 from jax import lax
 from jax.sharding import PartitionSpec as P
+
+
+def gather_around(x, axis, dim):
+    ways = lax.axis_size(axis)
+    up = [(d, (d + 1) % ways) for d in range(ways)]
+    down = [(d, (d - 1) % ways) for d in range(ways)]
+    earlier, later = ([x], [x])
+    for _ in range(ways // 2):
+        earlier.append(lax.ppermute(earlier[-1], axis, up))
+    for _ in range((ways - 1) // 2):
+        later.append(lax.ppermute(later[-1], axis, down))
+    line = jnp.concatenate([*earlier[::-1], *later[1:]], axis=dim)
+    return jnp.roll(line, (lax.axis_index(axis) - ways // 2) * x.shape[dim], axis=dim)
 
 
 def local(low_rhs, low_inv, low_tiles, tile_rows, tile_cols, top_rhs, top_inv, top_tiles):
@@ -47,7 +60,7 @@
         solved_part = jnp.dot(
             top_inv[level], whole_residue, preferred_element_type=jnp.float32
         ).astype(jnp.bfloat16)
-        top_forward.append(lax.all_gather(solved_part, "row", axis=0, tiled=True))
+        top_forward.append(gather_around(solved_part, "row", 0))
     for level in reversed(range(levels)):
         update = lax.dynamic_slice_in_dim(top_forward[level], position * share, share, 0).astype(
             jnp.float32

time: 906 us -> 892 us (0.985)
  blocking collectives: 253 us -> 131 us
  starting transfers between devices: 0.41 us -> 64.7 us
  waiting for transfers between devices: 596 us -> 630 us
    all_gather x4 -> x0, blocking collectives: 122 us -> none  [local(): top_forward.append(lax.all_gather(solved_part, 'row', axis=0, tiled=True))]
    ppermute x0 -> x28, starting transfers between devices: none -> 64.3 us  [the longest x12 56.8 us: gather_around(): later.append(lax.ppermute(later[-1], axis, down))]
    ppermute x0 -> x28, waiting for transfers between devices: none -> 38.6 us  [the longest x16 38.4 us: gather_around(): earlier.append(lax.ppermute(earlier[-1], axis, up))]
  transfers between devices with their start and end apart: 10 -> 38, of which waited for: 10 -> 27; matrix products, arithmetic and copies ran while one was open for 0% -> 1% of each run, Pallas kernels for 0% -> 0%
where the time goes in v1:
time: 892 us; the launch traced here: 890 us
  waiting for transfers between devices  630 us (71%)
  blocking collectives  131 us (15%)
  starting transfers between devices  64.7 us (7%)
  matrix products  24.6 us (3%)
  local copies, waits for them, and re-layouts  17.6 us (2%)
  between operations  15.2 us (2%)
    psum x4, waiting for transfers between devices, local(): lax.psum(local_part.astype(jnp.bfloat16), 'row').astype(jnp.float32)  282 us
    reduce_scatter x3, waiting for transfers between devices, local(): lax.psum_scatter(partial_term.astype(jnp.bfloat16), 'row', scatter_dimens...  185 us
    all_gather x4, blocking collectives, local(): lax.all_gather(residue.astype(jnp.bfloat16), 'row', axis=0, tiled=True)  123 us
    unnamed x11, waiting for transfers between devices  72.5 us
    ppermute x12, starting transfers between devices, gather_around(): later.append(lax.ppermute(later[-1], axis, down))  56.8 us
    ppermute x16, waiting for transfers between devices, gather_around(): earlier.append(lax.ppermute(earlier[-1], axis, up))  38.4 us
    psum x1, waiting for transfers between devices, local(): whole_sum = lax.psum(coupling.astype(jnp.bfloat16), 'col')  32.1 us
    reduce_scatter x1, waiting for transfers between devices, local(): lax.psum_scatter(terms.astype(jnp.bfloat16), 'col', scatter_dimension=0,...  19 us
  transfers between devices with their start and end apart: 38, of which 27 were waited for; matrix products, arithmetic and copies ran while one was open for 1% of the time, Pallas kernels for 0%

profile of v1, /device:TPU:0, one launch (start us, length us, event | category | flops | bytes accessed | tf_op | source)
XLA Modules:
  0.0 890.1 jit_solution(7792175258752948883)
XLA Ops:
  8.7 8.7 all-gather
  27.3 72.4 %all-reduce.18.cloned.1.call-done = bf16[4,512,128]{2,0,1:T(4,128)(2,1)} async-done(((bf16[4,512,128]{2,0,1:T(4,128)(2,1)}), bf16[4,512,128]{2,0,1:T(4,128)(2,1)}) %all-reduce.18.cloned.1.call-update) | async-done | bytes 524304
  101.2 32.1 %all-reduce.16.cloned.1.call-done = bf16[4,64,128]{2,1,0:T(8,128)(2,1)} async-done(((bf16[4,64,128]{2,1,0:T(8,128)(2,1)}), bf16[4,64,128]{2,1,0:T(8,128)(2,1)}) %all-reduce.16.cloned.1.call-update) | async-done | bytes 65552 | tf_op jit(solution)/shard_map/psum | solution.py:41
  134.1 30.7 %all-gather.1 = bf16[1,512,128]{2,1,0:T(8,128)(2,1)S(1)} all-gather(bf16[1,64,128]{2,1,0:T(8,128)(2,1)S(1)} %fusion.81), channel_id=3, replica_groups=mesh['row'=8,'col'=4] {'row'}, dimensions={1}, use_global_device_ids=true | all-gather | bytes 147456 | tf_op jit(solution)/shard_map/all_gather | solution.py:59
  166.4 5.0 collective-permute-done
  171.4 4.7 collective-permute-start.4
  177.9 4.7 collective-permute-start.5
  184.3 4.7 collective-permute-start.6
  191.4 30.5 %all_gather.17 = bf16[512,128]{1,0:T(8,128)(2,1)S(1)} all-gather(bf16[64,128]{1,0:T(8,128)(2,1)S(1)} %fusion.20), channel_id=1, replica_groups=mesh['row'=8,'col'=4] {'row'}, dimensions={0}, use_global_device_ids=true | all-gather | bytes 147456 | tf_op jit(solution)/shard_map/all_gather | solution.py:59
  235.0 4.7 collective-permute-start.12
  241.9 4.8 collective-permute-start.13
  249.5 30.8 %all_gather.18 = bf16[512,128]{1,0:T(8,128)(2,1)S(1)} all-gather(bf16[64,128]{1,0:T(8,128)(2,1)S(1)} %fusion.22), channel_id=1, replica_groups=mesh['row'=8,'col'=4] {'row'}, dimensions={0}, use_global_device_ids=true | all-gather | bytes 147456 | tf_op jit(solution)/shard_map/all_gather | solution.py:59
  293.5 4.7 collective-permute-start.19
  299.9 4.7 collective-permute-start.20
  307.8 30.7 %all_gather.19 = bf16[512,128]{1,0:T(8,128)(2,1)S(1)} all-gather(bf16[64,128]{1,0:T(8,128)(2,1)S(1)} %fusion.21), channel_id=1, replica_groups=mesh['row'=8,'col'=4] {'row'}, dimensions={0}, use_global_device_ids=true | all-gather | bytes 147456 | tf_op jit(solution)/shard_map/all_gather | solution.py:59
  358.0 4.8 collective-permute-start.27
  369.9 67.1 %all-reduce.8.cloned.1.call-done = bf16[512,128]{0,1:T(8,128)(2,1)} async-done(((bf16[512,128]{0,1:T(8,128)(2,1)}), bf16[512,128]{0,1:T(8,128)(2,1)}) %all-reduce.8.cloned.1.call-update) | async-done | bytes 131088 | tf_op jit(solution)/shard_map/psum | solution.py:86
  438.8 62.9 %reduce-scatter.5.cloned.1.call-done = bf16[64,128]{1,0:T(8,128)(2,1)} async-done(((bf16[512,128]{1,0:T(8,128)(2,1)}), bf16[64,128]{1,0:T(8,128)(2,1)}) %reduce-scatter.5.cloned.1.call-update) | async-done | bytes 16400 | tf_op jit(solution)/shard_map/reduce_scatter | solution.py:77
  503.6 71.5 %all-reduce.10.cloned.1.call-done = bf16[512,128]{0,1:T(8,128)(2,1)} async-done(((bf16[512,128]{0,1:T(8,128)(2,1)}), bf16[512,128]{0,1:T(8,128)(2,1)}) %all-reduce.10.cloned.1.call-update) | async-done | bytes 131088 | tf_op jit(solution)/shard_map/psum | solution.py:86
  578.3 61.5 %reduce-scatter.7.cloned.1.call-done = bf16[64,128]{1,0:T(8,128)(2,1)} async-done(((bf16[512,128]{1,0:T(8,128)(2,1)}), bf16[64,128]{1,0:T(8,128)(2,1)}) %reduce-scatter.7.cloned.1.call-update) | async-done | bytes 16400 | tf_op jit(solution)/shard_map/reduce_scatter | solution.py:77
  641.6 71.8 %all-reduce.12.cloned.1.call-done = bf16[512,128]{0,1:T(8,128)(2,1)} async-done(((bf16[512,128]{0,1:T(8,128)(2,1)}), bf16[512,128]{0,1:T(8,128)(2,1)}) %all-reduce.12.cloned.1.call-update) | async-done | bytes 131088 | tf_op jit(solution)/shard_map/psum | solution.py:86
  717.3 60.9 %reduce-scatter.9.cloned.1.call-done = bf16[64,128]{1,0:T(8,128)(2,1)} async-done(((bf16[512,128]{1,0:T(8,128)(2,1)}), bf16[64,128]{1,0:T(8,128)(2,1)}) %reduce-scatter.9.cloned.1.call-update) | async-done | bytes 16400 | tf_op jit(solution)/shard_map/reduce_scatter | solution.py:77
  780.0 71.7 %all-reduce.14.cloned.1.call-done = bf16[512,128]{0,1:T(8,128)(2,1)} async-done(((bf16[512,128]{0,1:T(8,128)(2,1)}), bf16[512,128]{0,1:T(8,128)(2,1)}) %all-reduce.14.cloned.1.call-update) | async-done | bytes 131088 | tf_op jit(solution)/shard_map/psum | solution.py:86
  862.3 19.0 %reduce-scatter.11.cloned.1.call-done = bf16[1,512,128]{2,1,0:T(8,128)(2,1)} async-done(((bf16[4,512,128]{2,1,0:T(8,128)(2,1)}), bf16[1,512,128]{2,1,0:T(8,128)(2,1)}) %reduce-scatter.11.cloned.1.call-update) | async-done | bytes 131088 | tf_op jit(solution)/shard_map/reduce_scatter | solution.py:97
  (191 shorter events, 109.7 us)
Async XLA Ops:
  7.2 92.4 %all-reduce.18.cloned.1.call-start = ((), (), s32[]{:S(2)}) async-start(), calls=%async_computation.13 | async-start | bytes 1048576
  26.0 107.3 %all-reduce.16.cloned.1.call-start = ((), (), s32[]{:S(2)}) async-start(), calls=%async_computation.12 | async-start | bytes 131072 | tf_op jit(solution)/shard_map/psum | solution.py:41
  101.1 335.9 %all-reduce.8.cloned.1.call-start = ((), (), s32[]{:S(2)}) async-start(), calls=%async_computation.4 | async-start | bytes 262144 | tf_op jit(solution)/shard_map/psum | solution.py:86
  164.9 6.5 collective-permute-start
  171.4 6.4 collective-permute-start.1
  171.4 6.4 collective-permute-start.4
  184.3 6.5 collective-permute-start.6
  222.1 6.5 collective-permute-start.7
  228.6 6.4 collective-permute-start.11
  235.0 6.9 collective-permute-start.12
  280.5 6.5 collective-permute-start.14
  287.0 6.4 collective-permute-start.18
  299.9 6.5 collective-permute-start.20
  338.6 6.5 collective-permute-start.21
  345.1 6.4 collective-permute-start.25
  358.0 6.5 collective-permute-start.24
  358.0 10.9 %collective-permute-start.27 = (bf16[64,128]{1,0:T(8,128)(2,1)}, bf16[64,128]{1,0:T(8,128)(2,1)S(1)}, u32[]{:S(2)}, u32[]{:S(2)}) collective-permute-start(bf16[64,128]{1,0:T(8,128)(2,1)} %collective-permute-done.26), channel_id=1, source_target_pairs={{0,28},{4,0},{8,4},{12,8},{16,12},{20,16},{24,20},{28,24},{1,29},{... | collective-permute-start | bytes 49160 | tf_op jit(solution)/shard_map/ppermute | solution.py:15
  369.9 131.9 %reduce-scatter.5.cloned.1.call-start = ((), (), s32[]{:S(2)}) async-start(), calls=%async_computation.5 | async-start | bytes 147456 | tf_op jit(solution)/shard_map/reduce_scatter | solution.py:77
  438.8 136.3 %all-reduce.10.cloned.1.call-start = ((), (), s32[]{:S(2)}) async-start(), calls=%async_computation.6 | async-start | bytes 262144 | tf_op jit(solution)/shard_map/psum | solution.py:86
  503.4 136.4 %reduce-scatter.7.cloned.1.call-start = ((), (), s32[]{:S(2)}) async-start(), calls=%async_computation.7 | async-start | bytes 147456 | tf_op jit(solution)/shard_map/reduce_scatter | solution.py:77
  578.2 135.1 %all-reduce.12.cloned.1.call-start = ((), (), s32[]{:S(2)}) async-start(), calls=%async_computation.8 | async-start | bytes 262144 | tf_op jit(solution)/shard_map/psum | solution.py:86
  641.5 136.7 %reduce-scatter.9.cloned.1.call-start = ((), (), s32[]{:S(2)}) async-start(), calls=%async_computation.9 | async-start | bytes 147456 | tf_op jit(solution)/shard_map/reduce_scatter | solution.py:77
  715.9 135.8 %all-reduce.14.cloned.1.call-start = ((), (), s32[]{:S(2)}) async-start(), calls=%async_computation.10 | async-start | bytes 262144 | tf_op jit(solution)/shard_map/psum | solution.py:86
  779.9 101.4 %reduce-scatter.11.cloned.1.call-start = ((), (), s32[]{:S(2)}) async-start(), calls=%async_computation.11 | async-start | bytes 655360 | tf_op jit(solution)/shard_map/reduce_scatter | solution.py:97
  (33 other events, 2047.7 us)
Sparse Core Ops, SparseCore 0:
  26.1 73.4 all-reduce.17
  102.5 30.7 all-reduce.15
  370.0 66.9 all-reduce.7
  440.8 60.9 reduce-scatter.4
  505.5 69.5 all-reduce.9
  578.8 60.9 reduce-scatter.6
  643.8 69.5 all-reduce.11
  717.2 60.9 reduce-scatter.8
  782.2 69.5 all-reduce.13
  860.5 20.7 reduce-scatter.10
